TPU v7x, 512 devices: a whole 4x4x16 slice. The times are simulated.
512 devices in a mesh: dp: 64 (over z, x_hi, core), fsdp: 8 (over x_lo, y).
Axes of the slice: x: 4 (x_hi: 2, x_lo: 2; x = x_hi * 2 + x_lo), y: 4, z: 16, core: 2. Of those that a mesh axis runs over, the one named last changes fastest.
Arguments:
- states: bfloat16 [128, 512, 5120], P('dp', None, 'fsdp'), may hold values from -240 to 240
- valid_counts: int32 [128], P('dp'), may hold values from 32 to 512
- section_ids: int32 [128], replicated, may hold values from 0 to 63, never falling along the last dimension, each value on 1 to 6 neighbouring positions
- norm_gain: bfloat16 [5120], P('fsdp'), may hold values from 0.099609375 to 1.8984375
- head_weight: bfloat16 [5120, 2048], P('fsdp'), may hold values from -0.078125 to 0.078125
Outputs:
- embeddings: float32 [64, 3840], P('dp')
Inputs may be any that keep to these rules, and one draw needn't show every extreme that they name: `section_ids`: section numbers never fall along the spans; every one of the 64 sections has 1 to 6 spans.
All inputs are finite; a program needn't handle non-finite values.
Results may differ from a plain program's by a relative error of at most 0.0003.
Values sent between devices are 32-bit elements; how exact they have to be, the bound alone decides.
No kernel may reach another device: no remote copies, remote signals or barrier semaphores. Data moves between devices by JAX's collectives and lax.ppermute only.
A program may use at most 64 MiB of HBM per device.

v0:
```python
import jax
import jax.numpy as jnp
from jax import lax
from jax.sharding import PartitionSpec as P

D = 5120
epsilon = 1e-06


def nested(projected):
    width = projected.shape[1]
    pieces = []
    for level in (width // 8, width // 4, width // 2, width):
        front = projected[:, :level]
        pieces.append(front * lax.rsqrt(jnp.mean(front * front, axis=1, keepdims=True) + epsilon))
    return jnp.concatenate(pieces, axis=1)


def local(states, valid_counts, section_ids, norm_gain, head_weight):
    values = states.astype(jnp.float32)
    partial_squares = jnp.sum(values * values, axis=-1)
    squares = lax.psum(partial_squares, "fsdp")
    scale = lax.rsqrt(squares / D + epsilon)
    slots = jnp.arange(states.shape[1], dtype=jnp.int32)
    used = (slots[None, :] < valid_counts[:, None]).astype(jnp.float32)
    weights = scale * used
    sums = jnp.einsum("cl,cld->cd", weights, values, precision=lax.Precision.HIGHEST)
    pooled = (
        sums / valid_counts.astype(jnp.float32)[:, None] * norm_gain.astype(jnp.float32)[None, :]
    )
    groups = lax.axis_size("dp")
    local_spans = pooled.shape[0]
    sec_local = local_spans // 2
    total_sections = sec_local * groups
    me = lax.axis_index("dp")
    my_ids = lax.dynamic_slice_in_dim(section_ids, me * local_spans, local_spans, 0)
    labels = jnp.arange(total_sections, dtype=jnp.int32)
    contrib = jnp.zeros((total_sections, pooled.shape[1]), jnp.float32)
    for c in range(local_spans):
        contrib = contrib + jnp.where((labels == my_ids[c])[:, None], pooled[c][None, :], 0.0)
    received = lax.all_to_all(contrib, "dp", 0, 0, tiled=True)
    section_sums = jnp.sum(received.reshape(groups, sec_local, -1), axis=0)
    terms = jnp.dot(section_sums, head_weight.astype(jnp.float32), precision=lax.Precision.HIGHEST)
    projected = lax.psum(terms, "fsdp")
    return nested(projected)


def solution(mesh):
    in_specs = (P("dp", None, "fsdp"), P("dp"), P(), P("fsdp"), P("fsdp", None))
    out_specs = P("dp", None)
    return jax.shard_map(local, mesh=mesh, in_specs=in_specs, out_specs=out_specs, check_vma=False)
```

profile of v0, /device:TPU:8, one launch (start us, length us, event | category | flops | bytes accessed | tf_op | source)
XLA Modules:
  0.0 90.2 jit_solution(11067146023472021934)
XLA Ops:
  0.0 0.0 copy-start
  0.0 0.8 convert_element_type.12
  0.8 0.7 dynamic_slice.3
  1.5 0.6 fusion.5
  2.1 0.7 convert_element_type.13
  2.8 1.6 %multiply_reduce_fusion = f32[2,512]{1,0:T(2,128)S(1)} fusion(bf16[2,512,640]{2,1,0:T(8,128)(2,1)} %param.5), kind=kLoop, calls=%fused_computation | loop fusion | flops 1965056 | bytes 1314816 | tf_op jit(solution)/shard_map/reduce_sum | solution.py:21
  4.5 21.8 %psum.14 = f32[2,512]{1,0:T(2,128)S(1)} all-reduce(f32[2,512]{1,0:T(2,128)S(1)} %multiply_reduce_fusion), channel_id=1, replica_groups=mesh['dp'=64,'fsdp'=8] {'fsdp'}, use_global_device_ids=true, to_apply=%region_1.0 | all-reduce | flops 1024 | bytes 8192 | tf_op jit(solution)/shard_map/psum | solution.py:22
  26.2 0.7 fusion.2
  27.0 1.9 %fusion.3 = f32[2,1,640]{2,1,0:T(1,128)S(1)} fusion(bf16[2,512,640]{2,1,0:T(8,128)(2,1)} %param.5, f32[2,512,1]{1,0,2:T(2,128)S(1)} %fusion.2), kind=kOutput, calls=%fused_computation.10 | convolution fusion | flops 7864320 | bytes 1319936 | tf_op jit(solution)/shard_map/cl,cld->cd/dot_general | solution.py:27
  28.9 0.1 fusion.1
  29.0 1.3 %iota_compare_fusion = (pred[64]{0:T(512)(128)(4,1)S(1)}, pred[64]{0:T(512)(128)(4,1)S(1)}) fusion(s32[]{:T(128)} %bitcast.3, s32[]{:T(128)} %bitcast), kind=kLoop, calls=%fused_computation.21 | loop fusion | flops 128 | bytes 136 | tf_op jit(solution)/shard_map/eq | solution.py:40
  30.3 0.2 fusion
  30.6 32.8 %all_to_all.6 = f32[64,1,640]{2,1,0:T(1,128)S(1)} all-to-all(f32[64,1,640]{2,1,0:T(1,128)S(1)} %fusion), channel_id=1, replica_groups=mesh['dp'=64,'fsdp'=8] {'dp'}, dimensions={0} | all-to-all | bytes 327680 | tf_op jit(solution)/shard_map/all_to_all | solution.py:41
  63.4 0.1 reduce_sum.55
  63.6 0.0 copy-done
  63.6 1.1 %fusion.6 = f32[1,2048]{1,0:T(1,128)S(1)} fusion(f32[640,1]{0,1:T(1,128)S(1)} %reshape.153, bf16[640,2048]{1,0:T(8,128)(2,1)S(1)} %copy-done), kind=kOutput, calls=%fused_computation.24 | convolution fusion | flops 15728640 | bytes 2632192 | tf_op jit(solution)/shard_map/dot_general | solution.py:43
  64.7 19.6 %psum.15 = f32[1,2048]{1,0:T(1,128)S(1)} all-reduce(f32[1,2048]{1,0:T(1,128)S(1)} %fusion.6), channel_id=1, replica_groups=mesh['dp'=64,'fsdp'=8] {'fsdp'}, use_global_device_ids=true, to_apply=%region_3.4 | all-reduce | flops 2048 | bytes 16384 | tf_op jit(solution)/shard_map/psum | solution.py:44
  84.3 0.6 multiply_reduce_fusion.1
  84.9 0.7 multiply_reduce_fusion.2
  85.6 0.6 multiply_reduce_fusion.3
  86.2 0.6 multiply_reduce_fusion.4
  89.5 0.6 pad_maximum_fusion
  (6 shorter events, 0.1 us)
Async XLA Ops:
  0.0 63.6 %copy-start = (bf16[640,2048]{1,0:T(8,128)(2,1)S(1)}, bf16[640,2048]{1,0:T(8,128)(2,1)}, u32[]{:S(2)}) copy-start(bf16[640,2048]{1,0:T(8,128)(2,1)} %param.9) | copy-start | bytes 7864324
where the time goes:
time: 90.5 us; the launch traced here: 90.2 us
  blocking collectives  74.2 us (82%)
  other arithmetic  8.81 us (10%)
  matrix products  3.06 us (3%)
  between operations  2.77 us (3%)
  local copies, waits for them, and re-layouts  1.36 us (2%)
    all_to_all x1, blocking collectives, local(): received = lax.all_to_all(contrib, 'dp', 0, 0, tiled=True)  32.8 us
    psum x1, blocking collectives, local(): squares = lax.psum(partial_squares, 'fsdp')  21.8 us
    psum x1, blocking collectives, local(): projected = lax.psum(terms, 'fsdp')  19.6 us
    reduce_sum x4, other arithmetic, nested(): jnp.mean(front * front, axis=1, keepdims=True) + epsilon  2.53 us
    dot_general x1, matrix products, local(): jnp.einsum('cl,cld->cd', weights, values, precision=lax.Precision.HIGHEST)  1.94 us

commit v1 on v0

--- a/solution.py
+++ b/solution.py
@@ -5,6 +5,11 @@
 
 D = 5120
 epsilon = 1e-06
+
+
+def gather_and_add(block, mesh_axis):
+    parts = lax.all_gather(block, mesh_axis)
+    return jnp.sum(parts, axis=0)
 
 
 def nested(projected):
@@ -19,7 +24,7 @@
 def local(states, valid_counts, section_ids, norm_gain, head_weight):
     values = states.astype(jnp.float32)
     partial_squares = jnp.sum(values * values, axis=-1)
-    squares = lax.psum(partial_squares, "fsdp")
+    squares = gather_and_add(partial_squares, "fsdp")
     scale = lax.rsqrt(squares / D + epsilon)
     slots = jnp.arange(states.shape[1], dtype=jnp.int32)
     used = (slots[None, :] < valid_counts[:, None]).astype(jnp.float32)

time: 90.5 us -> 102 us (1.13)
  the two profiles are of different devices: /device:TPU:8 before, /device:TPU:2 now
where the time goes in v1:
time: 102 us; the launch traced here: 101 us
  blocking collectives  85.2 us (84%)
  other arithmetic  8.83 us (9%)
  matrix products  3.06 us (3%)
  between operations  2.77 us (3%)
  local copies, waits for them, and re-layouts  1.36 us (1%)
    all_to_all x1, blocking collectives, local(): received = lax.all_to_all(contrib, 'dp', 0, 0, tiled=True)  35.3 us
    all_gather x1, blocking collectives, gather_and_add(): parts = lax.all_gather(block, mesh_axis)  29.8 us
    psum x1, blocking collectives, local(): projected = lax.psum(terms, 'fsdp')  20.1 us
    reduce_sum x4, other arithmetic, nested(): jnp.mean(front * front, axis=1, keepdims=True) + epsilon  2.53 us

profile of v1, /device:TPU:2, one launch (start us, length us, event | category | flops | bytes accessed | tf_op | source)
XLA Modules:
  0.0 101.2 jit_solution(11956574383922496008)
XLA Ops:
  0.0 0.0 copy-start
  0.0 0.8 convert_element_type.12
  0.8 0.7 dynamic_slice.3
  1.5 0.6 fusion.5
  2.1 0.7 convert_element_type.13
  2.8 1.6 %multiply_reduce_fusion = f32[2,512]{1,0:T(2,128)S(1)} fusion(bf16[2,512,640]{2,1,0:T(8,128)(2,1)} %param.5), kind=kLoop, calls=%fused_computation | loop fusion | flops 1965056 | bytes 1314816 | tf_op jit(solution)/shard_map/reduce_sum | solution.py:26
  4.5 29.8 %all-gather.1 = f32[8,2,512]{2,1,0:T(2,128)S(1)} all-gather(f32[1,2,512]{2,1,0:T(2,128)S(1)} %bitcast.13), channel_id=2, replica_groups=mesh['dp'=64,'fsdp'=8] {'fsdp'}, dimensions={0}, use_global_device_ids=true | all-gather | bytes 36864 | tf_op jit(solution)/shard_map/all_gather | solution.py:11
  34.3 0.7 fusion.2
  35.0 1.9 %fusion.3 = f32[2,1,640]{2,1,0:T(1,128)S(1)} fusion(bf16[2,512,640]{2,1,0:T(8,128)(2,1)} %param.5, f32[2,512,1]{1,0,2:T(2,128)S(1)} %fusion.2), kind=kOutput, calls=%fused_computation.10 | convolution fusion | flops 7864320 | bytes 1319936 | tf_op jit(solution)/shard_map/cl,cld->cd/dot_general | solution.py:32
  36.9 0.1 fusion.1
  37.1 1.3 %iota_compare_fusion = (pred[64]{0:T(512)(128)(4,1)S(1)}, pred[64]{0:T(512)(128)(4,1)S(1)}) fusion(s32[]{:T(128)} %bitcast.4, s32[]{:T(128)} %bitcast), kind=kLoop, calls=%fused_computation.21 | loop fusion | flops 128 | bytes 136 | tf_op jit(solution)/shard_map/eq | solution.py:45
  38.4 0.2 fusion
  38.6 35.3 %all_to_all.6 = f32[64,1,640]{2,1,0:T(1,128)S(1)} all-to-all(f32[64,1,640]{2,1,0:T(1,128)S(1)} %fusion), channel_id=1, replica_groups=mesh['dp'=64,'fsdp'=8] {'dp'}, dimensions={0} | all-to-all | bytes 327680 | tf_op jit(solution)/shard_map/all_to_all | solution.py:46
  74.0 0.1 reduce_sum.65
  74.1 0.0 copy-done
  74.1 1.1 %fusion.6 = f32[1,2048]{1,0:T(1,128)S(1)} fusion(f32[640,1]{0,1:T(1,128)S(1)} %reshape.157, bf16[640,2048]{1,0:T(8,128)(2,1)S(1)} %copy-done), kind=kOutput, calls=%fused_computation.24 | convolution fusion | flops 15728640 | bytes 2632192 | tf_op jit(solution)/shard_map/dot_general | solution.py:48
  75.2 20.1 %psum.7 = f32[1,2048]{1,0:T(1,128)S(1)} all-reduce(f32[1,2048]{1,0:T(1,128)S(1)} %fusion.6), channel_id=1, replica_groups=mesh['dp'=64,'fsdp'=8] {'fsdp'}, use_global_device_ids=true, to_apply=%region_3.4 | all-reduce | flops 2048 | bytes 16384 | tf_op jit(solution)/shard_map/psum | solution.py:49
  95.3 0.6 multiply_reduce_fusion.1
  95.9 0.7 multiply_reduce_fusion.2
  96.6 0.6 multiply_reduce_fusion.3
  97.2 0.6 multiply_reduce_fusion.4
  100.6 0.6 pad_maximum_fusion
  (7 shorter events, 0.1 us)
Async XLA Ops:
  0.0 74.1 %copy-start = (bf16[640,2048]{1,0:T(8,128)(2,1)S(1)}, bf16[640,2048]{1,0:T(8,128)(2,1)}, u32[]{:S(2)}) copy-start(bf16[640,2048]{1,0:T(8,128)(2,1)} %param.9) | copy-start | bytes 7864324
